TPU v7x, 32 devices: a whole 2x2x4 slice. The times are simulated.
32 devices in a mesh: dp: 4 (over y, core), row: 2 (over x), col: 4 (over z).
Axes of the slice: x: 2, y: 2, z: 4, core: 2. Of those that a mesh axis runs over, the one named last changes fastest.
Arguments:
- block_in: bfloat16 [8192, 1536], P(('dp', 'row', 'col')), may hold values from -6 to 6
- out_grad: bfloat16 [8192, 1536], P(('dp', 'row', 'col')), may hold values from -6 to 6
- norm_gain: float32 [1536], replicated, may hold values from 0.5 to 1.5
- first_norm_gain: float32 [1536], replicated, may hold values from -28 to 28
- second_norm_gain: float32 [1536], replicated, may hold values from 16.384 to 163.84
- input_proj: float32 [1536, 6144], P('dp', ('row', 'col')), may hold values from -0.18371173 to 0.18371173
- first_input_proj: float32 [1536, 6144], P('dp', ('row', 'col')), may hold values from -28 to 28
- second_input_proj: float32 [1536, 6144], P('dp', ('row', 'col')), may hold values from 16.384 to 163.84
- state_proj: float32 [1536, 256], P(('dp', 'row', 'col')), may hold values from -0.15625 to 0.15625
- first_state_proj: float32 [1536, 256], P(('dp', 'row', 'col')), may hold values from -28 to 28
- second_state_proj: float32 [1536, 256], P(('dp', 'row', 'col')), may hold values from 16.384 to 163.84
- step_proj: float32 [1536, 48], P(('dp', 'row', 'col')), may hold values from -0.15625 to 0.15625
- first_step_proj: float32 [1536, 48], P(('dp', 'row', 'col')), may hold values from -28 to 28
- second_step_proj: float32 [1536, 48], P(('dp', 'row', 'col')), may hold values from 16.384 to 163.84
- conv_taps: float32 [5, 3328], replicated, may hold values from -0.5 to 0.5
- first_conv_taps: float32 [5, 3328], replicated, may hold values from -28 to 28
- second_conv_taps: float32 [5, 3328], replicated, may hold values from 16.384 to 163.84
- head_coef: float32 [3, 48], replicated, may hold values from -7 to 3
- first_head_coef: float32 [3, 48], replicated, may hold values from -28 to 28
- second_head_coef: float32 [3, 48], replicated, may hold values from 16.384 to 163.84
- gated_gain: float32 [3072], replicated, may hold values from 0.5 to 1.5
- first_gated_gain: float32 [3072], replicated, may hold values from -28 to 28
- second_gated_gain: float32 [3072], replicated, may hold values from 16.384 to 163.84
- output_proj: float32 [3072, 1536], P(('row', 'col'), 'dp'), may hold values from -0.109375 to 0.109375
- first_output_proj: float32 [3072, 1536], P(('row', 'col'), 'dp'), may hold values from -28 to 28
- second_output_proj: float32 [3072, 1536], P(('row', 'col'), 'dp'), may hold values from 16.384 to 163.84
Outputs:
- block_out: bfloat16 [8192, 1536], P(('dp', 'row', 'col'))
- input_grad: float32 [8192, 1536], P(('dp', 'row', 'col'))
- grad_norm_gain: float32 [1536], replicated
- grad_input_proj: float32 [1536, 6144], P('dp', ('row', 'col'))
- grad_state_proj: float32 [1536, 256], P(('dp', 'row', 'col'))
- grad_step_proj: float32 [1536, 48], P(('dp', 'row', 'col'))
- grad_conv_taps: float32 [5, 3328], replicated
- grad_head_coef: float32 [3, 48], replicated
- grad_gated_gain: float32 [3072], replicated
- grad_output_proj: float32 [3072, 1536], P(('row', 'col'), 'dp')
- new_norm_gain: float32 [1536], replicated
- new_first_norm_gain: float32 [1536], replicated
- new_second_norm_gain: float32 [1536], replicated
- new_input_proj: float32 [1536, 6144], P('dp', ('row', 'col'))
- new_first_input_proj: float32 [1536, 6144], P('dp', ('row', 'col'))
- new_second_input_proj: float32 [1536, 6144], P('dp', ('row', 'col'))
- new_state_proj: float32 [1536, 256], P(('dp', 'row', 'col'))
- new_first_state_proj: float32 [1536, 256], P(('dp', 'row', 'col'))
- new_second_state_proj: float32 [1536, 256], P(('dp', 'row', 'col'))
- new_step_proj: float32 [1536, 48], P(('dp', 'row', 'col'))
- new_first_step_proj: float32 [1536, 48], P(('dp', 'row', 'col'))
- new_second_step_proj: float32 [1536, 48], P(('dp', 'row', 'col'))
- new_conv_taps: float32 [5, 3328], replicated
- new_first_conv_taps: float32 [5, 3328], replicated
- new_second_conv_taps: float32 [5, 3328], replicated
- new_head_coef: float32 [3, 48], replicated
- new_first_head_coef: float32 [3, 48], replicated
- new_second_head_coef: float32 [3, 48], replicated
- new_gated_gain: float32 [3072], replicated
- new_first_gated_gain: float32 [3072], replicated
- new_second_gated_gain: float32 [3072], replicated
- new_output_proj: float32 [3072, 1536], P(('row', 'col'), 'dp')
- new_first_output_proj: float32 [3072, 1536], P(('row', 'col'), 'dp')
- new_second_output_proj: float32 [3072, 1536], P(('row', 'col'), 'dp')
All inputs are finite; a program needn't handle non-finite values.
Results may differ from a plain program's by a relative error of at most 0.0034.
The roundings to bfloat16 on the way count: a program that leaves them out, or rounds other values in their place, can miss the bound.
Values may be sent and summed in bfloat16 or wider, within the bound.
No kernel may reach another device: no remote copies, remote signals or barrier semaphores. Data moves between devices by JAX's collectives and lax.ppermute only.
A program may use at most 192 MiB of HBM per device.

v0:
```python
import jax
import jax.numpy as jnp
from jax import lax
from jax.sharding import PartitionSpec as P

SPAN = 256
SEQ_LEN = 1024
ADAM_STEP = 4
PRECISE = lax.Precision.HIGHEST
NORM_EPS = 1e-05
BETA_ONE = 0.9
BETA_TWO = 0.95
ADAM_EPS = 1e-08
MATRIX_RATE = 0.003
VECTOR_RATE = 0.1
WEIGHT_DECAY = 0.1


def causal_conv(values, filters):
    length = values.shape[0]
    padded = jnp.pad(values, ((3, 0), (0, 0)))
    summed = filters[4][None, :] + jnp.zeros_like(values)
    for offset in range(4):
        summed = summed + filters[offset][None, :] * padded[offset : offset + length]
    return summed


def span_scan(values, deltas, rates, key_rows, query_rows):
    length, head_count, head_width = values.shape
    states = key_rows.shape[1]
    blocks = length // SPAN
    values = values.reshape(blocks, SPAN, head_count, head_width)
    deltas = deltas.reshape(blocks, SPAN, head_count)
    key_rows = key_rows.reshape(blocks, SPAN, states)
    query_rows = query_rows.reshape(blocks, SPAN, states)
    log_decay = jnp.cumsum(deltas * rates[None, None, :], axis=1)
    scores = jnp.einsum("kqn,krn->kqr", query_rows, key_rows, precision=PRECISE)
    causal = jnp.arange(SPAN)[:, None] >= jnp.arange(SPAN)[None, :]
    head_decay = jnp.transpose(log_decay, (0, 2, 1))
    head_deltas = jnp.transpose(deltas, (0, 2, 1))
    spread = head_decay[:, :, :, None] - head_decay[:, :, None, :]
    decays = jnp.exp(jnp.where(causal[None, None, :, :], spread, -jnp.inf))
    mixing = scores[:, None, :, :] * decays * head_deltas[:, :, None, :]
    within = jnp.einsum("khqr,krhp->kqhp", mixing, values, precision=PRECISE)
    to_end = jnp.exp(log_decay[:, -1:, :] - log_decay) * deltas
    produced = jnp.einsum("kqn,kqh,kqhp->khnp", key_rows, to_end, values, precision=PRECISE)
    factors = jnp.exp(log_decay[:, -1, :])
    carried = jnp.zeros((head_count, states, head_width), jnp.float32)
    entering = []
    for number in range(blocks):
        entering.append(carried)
        carried = carried * factors[number][:, None, None] + produced[number]
    entering = jnp.stack(entering)
    across = (
        jnp.einsum("kqn,khnp->kqhp", query_rows, entering, precision=PRECISE)
        * jnp.exp(log_decay)[:, :, :, None]
    )
    return (within + across).reshape(length, head_count, head_width)


def mixer_sequence(gate_part, inputs, state_in, step_raw, conv_inner, conv_state, coefs):
    length = inputs.shape[0]
    head_count = coefs.shape[1]
    head_width = inputs.shape[1] // head_count
    state_size = state_in.shape[1] // 2
    conv_out = jax.nn.silu(causal_conv(inputs, conv_inner))
    state_out = jax.nn.silu(causal_conv(state_in, conv_state))
    deltas = jax.nn.softplus(step_raw + coefs[0][None, :])
    rates = -jnp.exp(coefs[1])
    shaped = conv_out.reshape(length, head_count, head_width)
    result = span_scan(shaped, deltas, rates, state_out[:, :state_size], state_out[:, state_size:])
    result = result + coefs[2][None, :, None] * shaped
    return result.reshape(length, head_count * head_width) * jax.nn.silu(gate_part)


def mixer_all(gate_part, inputs, state_in, step_raw, conv_inner, conv_state, coefs):
    seq_count = inputs.shape[0] // SEQ_LEN

    def sequence(pieces):
        return mixer_sequence(
            pieces[0], pieces[1], pieces[2], pieces[3], conv_inner, conv_state, coefs
        )

    gated = lax.map(
        jax.checkpoint(sequence),
        (
            gate_part.reshape(seq_count, SEQ_LEN, -1),
            inputs.reshape(seq_count, SEQ_LEN, -1),
            state_in.reshape(seq_count, SEQ_LEN, -1),
            step_raw.reshape(seq_count, SEQ_LEN, -1),
        ),
    )
    return gated.reshape(inputs.shape[0], -1)


def adamw(weight, gradient, moment_one, moment_two, step_rate, shrink):
    new_one = BETA_ONE * moment_one + (1.0 - BETA_ONE) * gradient
    new_two = BETA_TWO * moment_two + (1.0 - BETA_TWO) * gradient * gradient
    one_hat = new_one / (1.0 - BETA_ONE**ADAM_STEP)
    two_hat = new_two / (1.0 - BETA_TWO**ADAM_STEP)
    updated = weight - step_rate * (one_hat / (jnp.sqrt(two_hat) + ADAM_EPS) + shrink * weight)
    return (updated, new_one, new_two)


def per_device(
    block_in,
    out_grad,
    norm_gain,
    first_norm_gain,
    second_norm_gain,
    input_proj,
    first_input_proj,
    second_input_proj,
    state_proj,
    first_state_proj,
    second_state_proj,
    step_proj,
    first_step_proj,
    second_step_proj,
    conv_taps,
    first_conv_taps,
    second_conv_taps,
    head_coef,
    first_head_coef,
    second_head_coef,
    gated_gain,
    first_gated_gain,
    second_gated_gain,
    output_proj,
    first_output_proj,
    second_output_proj,
):
    groups = lax.axis_size(("row", "col"))
    place = lax.axis_index(("row", "col"))
    tok_dev = block_in.shape[0]
    group_tok = tok_dev * groups
    inner = gated_gain.shape[0]
    inner_dev = inner // groups
    head_total = head_coef.shape[1]
    heads_dev = head_total // groups
    head_width = inner // head_total
    in_local, out_local = (
        lax.all_gather(input_proj.astype(jnp.bfloat16), "dp", axis=0, tiled=True),
        lax.all_gather(output_proj.astype(jnp.bfloat16), "dp", axis=1, tiled=True),
    )
    state_full, step_full = (
        lax.all_gather(state_proj.astype(jnp.bfloat16), ("dp", "row", "col"), axis=0, tiled=True),
        lax.all_gather(step_proj.astype(jnp.bfloat16), ("dp", "row", "col"), axis=0, tiled=True),
    )
    x_float = block_in.astype(jnp.float32)
    inv_rms = lax.rsqrt(jnp.mean(x_float * x_float, axis=1, keepdims=True) + NORM_EPS)
    normed_in = (x_float * inv_rms * norm_gain[None, :]).astype(jnp.bfloat16)
    state_own = jnp.dot(normed_in, state_full, preferred_element_type=jnp.float32).astype(
        jnp.bfloat16
    )
    step_own = jnp.dot(normed_in, step_full, preferred_element_type=jnp.float32).astype(
        jnp.bfloat16
    )
    normed_all, state_all, step_all, cotangent = (
        lax.all_gather(normed_in, ("row", "col"), axis=0, tiled=True),
        lax.all_gather(state_own, ("row", "col"), axis=0, tiled=True),
        lax.all_gather(step_own, ("row", "col"), axis=0, tiled=True),
        lax.all_gather(out_grad, ("row", "col"), axis=0, tiled=True),
    )
    projected = jnp.dot(normed_all, in_local, preferred_element_type=jnp.float32)
    paired = projected.reshape(group_tok, heads_dev, 2, head_width)
    gate_part = paired[:, :, 0, :].reshape(group_tok, inner_dev)
    inputs = paired[:, :, 1, :].reshape(group_tok, inner_dev)
    conv_inner = lax.dynamic_slice_in_dim(conv_taps, place * inner_dev, inner_dev, 1)
    conv_state = conv_taps[:, inner:]
    coefs = lax.dynamic_slice_in_dim(head_coef, place * heads_dev, heads_dev, 1)
    step_local = lax.dynamic_slice_in_dim(step_all, place * heads_dev, heads_dev, 1).astype(
        jnp.float32
    )
    gated, mixer_pull = jax.vjp(
        mixer_all,
        gate_part,
        inputs,
        state_all.astype(jnp.float32),
        step_local,
        conv_inner,
        conv_state,
        coefs,
    )
    squares = lax.psum(jnp.sum(gated * gated, axis=1), ("row", "col"))
    gated_rms = lax.rsqrt(squares / inner + NORM_EPS)[:, None]
    gain_local = lax.dynamic_slice_in_dim(gated_gain, place * inner_dev, inner_dev, 0)
    normed_out = (gated * gated_rms * gain_local[None, :]).astype(jnp.bfloat16)
    rows = normed_out
    mixed = lax.psum_scatter(
        jnp.dot(rows, out_local, preferred_element_type=jnp.float32),
        ("row", "col"),
        scatter_dimension=0,
        tiled=True,
    )
    block_out = (x_float + mixed).astype(jnp.bfloat16)
    grad_out_local = jnp.einsum(
        "tc,td->cd", normed_out, cotangent, preferred_element_type=jnp.float32
    )
    d_normed = jnp.einsum("td,cd->tc", cotangent, out_local, preferred_element_type=jnp.float32)
    gain_part = jnp.sum(d_normed * gated * gated_rms, axis=0)
    scaled = d_normed * gain_local[None, :]
    cross = lax.psum(jnp.sum(scaled * gated, axis=1), ("row", "col"))
    d_gated = gated_rms * scaled - gated * gated_rms**3 * (cross / inner)[:, None]
    d_gate, d_inputs, d_state, d_step, d_conv_inner, d_conv_state, d_coefs = mixer_pull(d_gated)
    d_projected = (
        jnp.stack(
            [
                d_gate.reshape(group_tok, heads_dev, head_width),
                d_inputs.reshape(group_tok, heads_dev, head_width),
            ],
            axis=2,
        )
        .reshape(group_tok, 2 * inner_dev)
        .astype(jnp.bfloat16)
    )
    grad_in_local = jnp.einsum(
        "td,tc->dc", normed_all, d_projected, preferred_element_type=jnp.float32
    )
    rows = d_projected
    d_normed_in = lax.psum_scatter(
        jnp.einsum("tc,dc->td", rows, in_local, preferred_element_type=jnp.float32),
        ("row", "col"),
        scatter_dimension=0,
        tiled=True,
    )
    step_spread = lax.dynamic_update_slice_in_dim(
        jnp.zeros((group_tok, head_total), jnp.float32), d_step, place * heads_dev, 1
    )
    state_back, step_back = (
        lax.psum_scatter(d_state, ("row", "col"), scatter_dimension=0, tiled=True),
        lax.psum_scatter(step_spread, ("row", "col"), scatter_dimension=0, tiled=True),
    )
    state_back = state_back.astype(jnp.bfloat16)
    step_back = step_back.astype(jnp.bfloat16)
    d_normed_in = (
        d_normed_in
        + jnp.einsum("tc,dc->td", state_back, state_full, preferred_element_type=jnp.float32)
        + jnp.einsum("tc,dc->td", step_back, step_full, preferred_element_type=jnp.float32)
    )
    grad_state_part = jnp.einsum(
        "td,tc->dc", normed_in, state_back, preferred_element_type=jnp.float32
    )
    grad_step_part = jnp.einsum(
        "td,tc->dc", normed_in, step_back, preferred_element_type=jnp.float32
    )
    grad_state, grad_step = (
        lax.psum_scatter(grad_state_part, ("dp", "row", "col"), scatter_dimension=0, tiled=True),
        lax.psum_scatter(grad_step_part, ("dp", "row", "col"), scatter_dimension=0, tiled=True),
    )
    grad_input, grad_output = (
        lax.psum_scatter(grad_in_local, "dp", scatter_dimension=0, tiled=True),
        lax.psum_scatter(grad_out_local, "dp", scatter_dimension=1, tiled=True),
    )
    scaled_in = d_normed_in * norm_gain[None, :]
    norm_part = jnp.sum(d_normed_in * x_float * inv_rms, axis=0)
    input_grad = (
        out_grad.astype(jnp.float32)
        + inv_rms * scaled_in
        - x_float * inv_rms**3 * jnp.mean(scaled_in * x_float, axis=1, keepdims=True)
    )
    gated_spread = lax.dynamic_update_slice_in_dim(
        jnp.zeros((inner,), jnp.float32), gain_part, place * inner_dev, 0
    )
    conv_front = lax.dynamic_update_slice_in_dim(
        jnp.zeros((5, inner), jnp.float32), d_conv_inner, place * inner_dev, 1
    )
    conv_spread = jnp.concatenate([conv_front, d_conv_state], axis=1)
    coef_spread = lax.dynamic_update_slice_in_dim(
        jnp.zeros((3, head_total), jnp.float32), d_coefs, place * heads_dev, 1
    )
    grad_norm, grad_gated, grad_conv, grad_coef = lax.psum(
        (norm_part, gated_spread, conv_spread, coef_spread), ("dp", "row", "col")
    )
    n_norm, f_norm, s_norm = adamw(
        norm_gain, grad_norm, first_norm_gain, second_norm_gain, VECTOR_RATE, 0.0
    )
    n_input, f_input, s_input = adamw(
        input_proj, grad_input, first_input_proj, second_input_proj, MATRIX_RATE, WEIGHT_DECAY
    )
    n_state, f_state, s_state = adamw(
        state_proj, grad_state, first_state_proj, second_state_proj, MATRIX_RATE, WEIGHT_DECAY
    )
    n_step, f_step, s_step = adamw(
        step_proj, grad_step, first_step_proj, second_step_proj, MATRIX_RATE, WEIGHT_DECAY
    )
    n_conv, f_conv, s_conv = adamw(
        conv_taps, grad_conv, first_conv_taps, second_conv_taps, VECTOR_RATE, 0.0
    )
    n_head, f_head, s_head = adamw(
        head_coef, grad_coef, first_head_coef, second_head_coef, VECTOR_RATE, 0.0
    )
    n_gated, f_gated, s_gated = adamw(
        gated_gain, grad_gated, first_gated_gain, second_gated_gain, VECTOR_RATE, 0.0
    )
    n_output, f_output, s_output = adamw(
        output_proj, grad_output, first_output_proj, second_output_proj, MATRIX_RATE, WEIGHT_DECAY
    )
    return (
        block_out,
        input_grad,
        grad_norm,
        grad_input,
        grad_state,
        grad_step,
        grad_conv,
        grad_coef,
        grad_gated,
        grad_output,
        n_norm,
        f_norm,
        s_norm,
        n_input,
        f_input,
        s_input,
        n_state,
        f_state,
        s_state,
        n_step,
        f_step,
        s_step,
        n_conv,
        f_conv,
        s_conv,
        n_head,
        f_head,
        s_head,
        n_gated,
        f_gated,
        s_gated,
        n_output,
        f_output,
        s_output,
    )


def solution(mesh):
    return jax.shard_map(
        per_device,
        mesh=mesh,
        in_specs=(
            P(("dp", "row", "col"), None),
            P(("dp", "row", "col"), None),
            P(),
            P(),
            P(),
            P("dp", ("row", "col")),
            P("dp", ("row", "col")),
            P("dp", ("row", "col")),
            P(("dp", "row", "col"), None),
            P(("dp", "row", "col"), None),
            P(("dp", "row", "col"), None),
            P(("dp", "row", "col"), None),
            P(("dp", "row", "col"), None),
            P(("dp", "row", "col"), None),
            P(),
            P(),
            P(),
            P(),
            P(),
            P(),
            P(),
            P(),
            P(),
            P(("row", "col"), "dp"),
            P(("row", "col"), "dp"),
            P(("row", "col"), "dp"),
        ),
        out_specs=(
            P(("dp", "row", "col"), None),
            P(("dp", "row", "col"), None),
            P(),
            P("dp", ("row", "col")),
            P(("dp", "row", "col"), None),
            P(("dp", "row", "col"), None),
            P(),
            P(),
            P(),
            P(("row", "col"), "dp"),
            P(),
            P(),
            P(),
            P("dp", ("row", "col")),
            P("dp", ("row", "col")),
            P("dp", ("row", "col")),
            P(("dp", "row", "col"), None),
            P(("dp", "row", "col"), None),
            P(("dp", "row", "col"), None),
            P(("dp", "row", "col"), None),
            P(("dp", "row", "col"), None),
            P(("dp", "row", "col"), None),
            P(),
            P(),
            P(),
            P(),
            P(),
            P(),
            P(),
            P(),
            P(),
            P(("row", "col"), "dp"),
            P(("row", "col"), "dp"),
            P(("row", "col"), "dp"),
        ),
        check_vma=False,
    )
```

profile of v0, /device:TPU:0, one launch (start us, length us, event | category | flops | bytes accessed | tf_op | source)
XLA Modules:
  0.0 1698.1 jit_solution(3342387534222917837)
XLA Ops:
  10.1 77.2 %all_gather.26 = bf16[1536,256]{1,0:T(8,128)(2,1)S(1)} all-gather(bf16[48,256]{1,0:T(8,128)(2,1)S(1)} %convert_element_type.58), channel_id=1, replica_groups=mesh['dp'=4,'row'=2,'col'=4] {'dp','row','col'}, dimensions={0}, use_global_device_ids=true | all-gather | bytes 811008 | tf_op jit(solution)/shard_map/all_gather | solution.py:147
  95.0 68.2 %all_gather.28 = bf16[1536,48]{1,0:T(8,128)(2,1)S(1)} all-gather(bf16[48,48]{1,0:T(8,128)(2,1)S(1)} %convert_element_type.60), channel_id=1, replica_groups=mesh['dp'=4,'row'=2,'col'=4] {'dp','row','col'}, dimensions={0}, use_global_device_ids=true | all-gather | bytes 152064 | tf_op jit(solution)/shard_map/all_gather | solution.py:148
  164.0 32.7 %all_gather.29 = bf16[2048,48]{0,1:T(8,128)(2,1)S(1)} all-gather(bf16[256,48]{0,1:T(8,128)(2,1)S(1)} %convolution_convert_fusion.1), channel_id=1, replica_groups=mesh['dp'=4,'row'=2,'col'=4] {'row','col'}, dimensions={0}, use_global_device_ids=true | all-gather | bytes 221184 | tf_op jit(solution)/shard_map/all_gather | solution.py:162
  199.8 2.7 convert.12
  202.5 55.3 %all-gather.6.cloned.1.call-done = bf16[2048,1536]{1,0:T(8,128)(2,1)} async-done(((bf16[256,1536]{1,0:T(8,128)(2,1)}), bf16[2048,1536]{1,0:T(8,128)(2,1)}) %all-gather.6.cloned.1.call-update) | async-done | bytes 6291472 | tf_op jit(solution)/shard_map/all_gather | solution.py:160
  257.7 8.1 fusion.182
  265.9 3.3 slice_bitcast_fusion.6
  269.2 4.3 reshape_reshape_squeeze.7
  276.1 4.2 reshape_reshape_squeeze.6
  283.0 75.7 %while.43 = (s32[]{:T(128)}, f32[2,1024,384]{1,2,0:T(8,128)}, f32[1,384]{1,0:T(1,128)S(1)}, f32[2,1024,384]{1,2,0:T(8,128)}, f32[1,384]{1,0:T(1,128)S(1)}, /*ind...) while((s32[]{:T(128)}, f32[2,1024,384]{1,2,0:T(8,128)}, ...), condition=%wide.region_4.5_spmd.clone.clone, body=%wide.region_1.4_spmd.clone.sunk.clone | while | flops 2843105280 | bytes 111481648 | solution.py:84
  283.6 7.2 reduce-window.84
  296.9 2.7 divide_multiply_fusion.7
  306.8 7.2 bitcast_add_fusion.14
  321.3 7.2 reduce-window.84
  334.6 2.7 divide_multiply_fusion.7
  344.5 7.2 bitcast_add_fusion.14
  358.7 3.7 copy.355
  362.7 19.9 %psum.42 = f32[2048]{0:T(1024)S(1)} all-reduce(f32[2048]{0:T(1024)S(1)} %bitcast.754), channel_id=1, replica_groups=mesh['dp'=4,'row'=2,'col'=4] {'row','col'}, use_global_device_ids=true, to_apply=%region_6.7 | all-reduce | flops 2048 | bytes 16384 | tf_op jit(solution)/shard_map/psum | solution.py:185
  382.7 10.2 fusion.138
  392.9 18.0 %psum.43 = f32[2048]{0:T(1024)S(1)} all-reduce(f32[2048]{0:T(1024)S(1)} %get-tuple-element.979), channel_id=1, replica_groups=mesh['dp'=4,'row'=2,'col'=4] {'row','col'}, use_global_device_ids=true, to_apply=%region_9.10 | all-reduce | flops 2048 | bytes 16384 | tf_op jit(solution)/shard_map/psum | solution.py:203
  410.9 4.3 fusion.135
  417.3 292.8 %while.44 = (s32[]{:T(128)}, f32[5,384]{1,0:T(8,128)}, f32[5,256]{1,0:T(8,128)}, f32[3,6]{1,0:T(4,128)}, bf16[2,1024,384]{1,2,0:T(8,128)(2,1)}, /*index=5*/bf16[...) while((s32[]{:T(128)}, f32[5,384]{1,0:T(8,128)}, ...), condition=%wide.region_38.39_spmd.clone.clone, body=%wide.region_10.38_spmd.clone.sunk.clone | while | flops 8532760576 | bytes 316975616 | solution.py:84
  423.3 3.4 dynamic-slice_bitcast_fusion.21
  429.6 7.2 reduce-window.87
  441.4 4.3 fusion.372
  450.2 5.6 bitcast_add_fusion.15
  458.4 3.1 broadcast_multiply_fusion.22
  468.4 3.5 fusion.379
  474.4 2.8 fusion.381
  480.3 4.3 fusion.382
  488.1 8.8 bitcast_add_fusion.16
  496.9 9.6 fusion.380
  511.5 30.6 %reduce-window.88 = f32[4,6,2,128]{3,2,1,0:T(2,128)S(1)} reduce-window(f32[4,6,2,128]{3,2,1,0:T(2,128)S(1)} %reshape.763, f32[]{:T(128)} %constant.263.clone.1..sunk.3), window={size=1x1x1x128 pad=0_0x0_0x0_0x0_127}, to_apply=%region_33.33 | reduce-window | flops 780288 | bytes 49156 | tf_op jit(solution)/shard_map/reduce-window.36
  565.7 3.4 dynamic-slice_bitcast_fusion.21
  572.0 7.2 reduce-window.87
  583.8 4.3 fusion.372
  592.7 5.6 bitcast_add_fusion.15
  600.9 3.1 broadcast_multiply_fusion.22
  610.9 3.5 fusion.379
  616.8 2.8 fusion.381
  622.7 4.3 fusion.382
  630.6 9.0 bitcast_add_fusion.16
  639.5 9.6 fusion.380
  654.1 30.3 %reduce-window.88 = f32[4,6,2,128]{3,2,1,0:T(2,128)S(1)} reduce-window(f32[4,6,2,128]{3,2,1,0:T(2,128)S(1)} %reshape.763, f32[]{:T(128)} %constant.263.clone.1..sunk.3), window={size=1x1x1x128 pad=0_0x0_0x0_0x0_127}, to_apply=%region_33.33 | reduce-window | flops 780288 | bytes 49156 | tf_op jit(solution)/shard_map/reduce-window.36
  713.8 61.1 %reduce-scatter.15.cloned.1.call-done = f32[256,48]{0,1:T(8,128)} async-done(((f32[2048,48]{0,1:T(8,128)}), f32[256,48]{0,1:T(8,128)}) %reduce-scatter.15.cloned.1.call-update) | async-done | bytes 49168 | tf_op jit(solution)/shard_map/reduce_scatter | solution.py:232
  777.1 6.8 fusion.186
  784.0 62.0 %reduce-scatter.13.cloned.1.call-done = f32[256,256]{1,0:T(8,128)} async-done(((f32[2048,256]{1,0:T(8,128)}), f32[256,256]{1,0:T(8,128)}) %reduce-scatter.13.cloned.1.call-update) | async-done | bytes 262160 | tf_op jit(solution)/shard_map/reduce_scatter | solution.py:231
  848.6 4.2 copy.360
  852.8 3.9 reshape.654
  856.7 4.2 copy.361
  860.9 3.8 reshape.655
  869.0 8.8 fusion.185
  877.8 10.4 fusion.184
  889.4 6.4 fusion.183
  896.9 76.9 %all-reduce.38.cloned.1.call-done = f32[5,3328]{1,0:T(8,128)} async-done(((f32[5,3328]{1,0:T(8,128)}), f32[5,3328]{1,0:T(8,128)}) %all-reduce.38.cloned.1.call-update) | async-done | bytes 66576 | tf_op jit(solution)/shard_map/psum | solution.py:272
  975.5 101.2 %reduce-scatter.21.cloned.1.call-done = f32[48,48]{1,0:T(8,128)} async-done(((f32[1536,48]{1,0:T(8,128)}), f32[48,48]{1,0:T(8,128)}) %reduce-scatter.21.cloned.1.call-update) | async-done | bytes 9232 | tf_op jit(solution)/shard_map/reduce_scatter | solution.py:249
  1078.0 33.4 %reduce-scatter.23.cloned.1.call-done = f32[384,384]{1,0:T(8,128)} async-done(((f32[384,1536]{1,0:T(8,128)}), f32[384,384]{1,0:T(8,128)}) %reduce-scatter.23.cloned.1.call-update) | async-done | bytes 589840 | tf_op jit(solution)/shard_map/reduce_scatter | solution.py:253
  1114.0 101.3 %reduce-scatter.19.cloned.1.call-done = f32[48,256]{1,0:T(8,128)} async-done(((f32[1536,256]{1,0:T(8,128)}), f32[48,256]{1,0:T(8,128)}) %reduce-scatter.19.cloned.1.call-update) | async-done | bytes 49168 | tf_op jit(solution)/shard_map/reduce_scatter | solution.py:248
  1216.7 48.5 %reduce-scatter.17.cloned.1.call-done = f32[384,768]{1,0:T(8,128)} async-done(((f32[1536,768]{1,0:T(8,128)}), f32[384,768]{1,0:T(8,128)}) %reduce-scatter.17.cloned.1.call-update) | async-done | bytes 1179664 | tf_op jit(solution)/shard_map/reduce_scatter | solution.py:252
  1265.3 4.3 multiply_subtract_fusion
  1269.6 206.7 %reduce-scatter.11.cloned.1.call-done = f32[256,1536]{1,0:T(8,128)} async-done(((f32[2048,1536]{1,0:T(8,128)}), f32[256,1536]{1,0:T(8,128)}) %reduce-scatter.11.cloned.1.call-update) | async-done | bytes 1572880 | tf_op jit(solution)/shard_map/reduce_scatter | solution.py:221
  1479.5 43.5 %all-reduce.35 = (f32[1536]{0:T(1024)S(1)}, f32[3,48]{1,0:T(4,128)S(1)}, f32[3072]{0:T(1024)S(1)}) all-reduce(f32[1536]{0:T(1024)S(1)} %get-tuple-element.980, f32[3,48]{1,0:T(4,128)} %copy-done.151, f32[3072]{0:T(1024)} %copy-done.141), channel_id=1, replica_groups=mesh['dp'=4,'row'=2,'col'=4] {'dp','row','col'}, use_global_device_ids=true, to_apply=%region_44.45 | all-reduce | flops 4752 | bytes 38016 | tf_op jit(solution)/shard_map/psum | solution.py:272
  1527.7 159.6 %reduce-scatter.9.cloned.1.call-done = f32[256,1536]{1,0:T(8,128)} async-done(((f32[2048,1536]{1,0:T(8,128)}), f32[256,1536]{1,0:T(8,128)}) %reduce-scatter.9.cloned.1.call-update) | async-done | bytes 1572880 | tf_op jit(solution)/shard_map/reduce_scatter | solution.py:190
  1687.3 3.4 fusion.144
  (853 shorter events, 208.2 us)
Async XLA Ops:
  7.2 80.1 %copy-start.51 = (bf16[256,1536]{1,0:T(8,128)(2,1)S(1)}, bf16[256,1536]{1,0:T(8,128)(2,1)}, u32[]{:S(2)}) copy-start(bf16[256,1536]{1,0:T(8,128)(2,1)} %param.30) | copy-start | bytes 2359300
  7.2 80.1 %copy-start.123 = (f32[1536]{0:T(1024)S(1)}, f32[1536]{0:T(1024)}, u32[]{:S(2)}) copy-start(f32[1536]{0:T(1024)} %param.32) | copy-start | bytes 18436
  7.2 192.5 %all-gather.10.cloned.1.call-start = ((), (), s32[]{:S(2)}) async-start(), calls=%async_computation.10 | async-start | bytes 1179648 | tf_op jit(solution)/shard_map/all_gather | solution.py:161
  9.3 78.0 %copy-start.146 = (f32[256]{0:T(256)}, f32[256]{0:T(256)S(1)}, u32[]{:S(2)}) copy-start(f32[256]{0:T(256)S(1)} %get-tuple-element.1168) | copy-start | bytes 3076
  88.7 113.8 %all-gather.8.cloned.1.call-start = ((), (), s32[]{:S(2)}) async-start(), calls=%async_computation.9 | async-start | bytes 2949120 | tf_op jit(solution)/shard_map/all_gather | solution.py:143
  90.1 167.6 %all-gather.6.cloned.1.call-start = ((), (), s32[]{:S(2)}) async-start(), calls=%async_computation.8 | async-start | bytes 7077888 | tf_op jit(solution)/shard_map/all_gather | solution.py:160
  90.8 291.8 %all-gather.12.cloned.1.call-start = ((), (), s32[]{:S(2)}) async-start(), calls=%async_computation.11 | async-start | bytes 1474560 | tf_op jit(solution)/shard_map/all_gather | solution.py:144
  91.7 71.6 %copy-start.34 = (bf16[256,1536]{1,0:T(8,128)(2,1)S(1)}, bf16[256,1536]{1,0:T(8,128)(2,1)}, u32[]{:S(2)}) copy-start(bf16[256,1536]{1,0:T(8,128)(2,1)} %copy-done.33) | copy-start | bytes 2359300
  91.7 291.0 %all-gather.14.cloned.1.call-start = ((), (), s32[]{:S(2)}) async-start(), calls=%async_computation.13 | async-start | bytes 7077888 | tf_op jit(solution)/shard_map/all_gather | solution.py:163
  92.3 682.6 %reduce-scatter.15.cloned.1.call-start = ((), (), s32[]{:S(2)}) async-start(), calls=%async_computation.16 | async-start | bytes 442368 | tf_op jit(solution)/shard_map/reduce_scatter | solution.py:232
  94.1 171.7 %copy-start.45 = (bf16[2,1024,384]{1,2,0:T(8,128)(2,1)}, bf16[2,1024,384]{1,2,0:T(8,128)(2,1)S(1)}, u32[]{:S(2)}) copy-start(bf16[2,1024,384]{1,2,0:T(8,128)(2,1)S(1)} %fusion.176) | copy-start | bytes 4718596
  382.7 28.2 %copy-start.53 = (f32[2,1024,384]{2,1,0:T(8,128)S(1)}, f32[2,1024,384]{2,1,0:T(8,128)}, u32[]{:S(2)}) copy-start(f32[2,1024,384]{2,1,0:T(8,128)} %copy.355) | copy-start | bytes 9437188
  417.7 10.3 copy-start.121
  417.7 10.4 copy-start.108
  418.3 10.4 copy-start.60
  423.3 15.5 copy-start.2
  427.9 12.7 copy-start.127
  428.1 13.3 copy-start.100
  428.1 13.3 copy-start.102
  428.1 13.3 copy-start.104
  428.1 13.3 copy-start.106
  560.1 10.3 copy-start.121
  560.1 10.4 copy-start.108
  560.7 10.4 copy-start.60
  565.7 15.5 copy-start.2
  570.3 12.7 copy-start.127
  570.5 13.3 copy-start.100
  570.5 13.3 copy-start.102
  570.5 13.3 copy-start.104
  570.5 13.3 copy-start.106
  710.2 64.7 %copy-start.35 = (bf16[256,1536]{1,0:T(8,128)(2,1)S(1)}, bf16[256,1536]{1,0:T(8,128)(2,1)}, u32[]{:S(2)}) copy-start(bf16[256,1536]{1,0:T(8,128)(2,1)} %copy-done.33) | copy-start | bytes 2359300
  712.2 133.8 %reduce-scatter.13.cloned.1.call-start = ((), (), s32[]{:S(2)}) async-start(), calls=%async_computation.15 | async-start | bytes 2359296 | tf_op jit(solution)/shard_map/reduce_scatter | solution.py:231
  713.0 64.1 %copy-start.43 = (bf16[2048,384]{1,0:T(8,128)(2,1)S(1)}, bf16[2048,384]{1,0:T(8,128)(2,1)}, u32[]{:S(2)}) copy-start(bf16[2048,384]{1,0:T(8,128)(2,1)} %get-tuple-element.1147) | copy-start | bytes 4718596
  713.0 260.8 %all-reduce.38.cloned.1.call-start = ((), (), s32[]{:S(2)}) async-start(), calls=%async_computation.20 | async-start | bytes 212992 | tf_op jit(solution)/shard_map/psum | solution.py:272
  713.8 362.9 %reduce-scatter.21.cloned.1.call-start = ((), (), s32[]{:S(2)}) async-start(), calls=%async_computation.19 | async-start | bytes 811008 | tf_op jit(solution)/shard_map/reduce_scatter | solution.py:249
  777.0 334.4 %reduce-scatter.23.cloned.1.call-start = ((), (), s32[]{:S(2)}) async-start(), calls=%async_computation.21 | async-start | bytes 2949120 | tf_op jit(solution)/shard_map/reduce_scatter | solution.py:253
  783.9 431.3 %reduce-scatter.19.cloned.1.call-start = ((), (), s32[]{:S(2)}) async-start(), calls=%async_computation.18 | async-start | bytes 1622016 | tf_op jit(solution)/shard_map/reduce_scatter | solution.py:248
  848.5 416.7 %reduce-scatter.17.cloned.1.call-start = ((), (), s32[]{:S(2)}) async-start(), calls=%async_computation.17 | async-start | bytes 5898240 | tf_op jit(solution)/shard_map/reduce_scatter | solution.py:252
  877.8 598.6 %reduce-scatter.11.cloned.1.call-start = ((), (), s32[]{:S(2)}) async-start(), calls=%async_computation.14 | async-start | bytes 14155776 | tf_op jit(solution)/shard_map/reduce_scatter | solution.py:221
  888.2 799.1 %reduce-scatter.9.cloned.1.call-start = ((), (), s32[]{:S(2)}) async-start(), calls=%async_computation.12 | async-start | bytes 14155776 | tf_op jit(solution)/shard_map/reduce_scatter | solution.py:190
  895.8 78.0 %copy-start.120 = (f32[5,3328]{1,0:T(8,128)S(1)}, f32[5,3328]{1,0:T(8,128)}, u32[]{:S(2)}) copy-start(f32[5,3328]{1,0:T(8,128)} %param.44) | copy-start | bytes 199684
  895.8 78.0 %copy-start.131 = (f32[5,3328]{1,0:T(8,128)S(1)}, f32[5,3328]{1,0:T(8,128)}, u32[]{:S(2)}) copy-start(f32[5,3328]{1,0:T(8,128)} %param.45) | copy-start | bytes 199684
  895.8 78.0 %copy-start.132 = (f32[5,3328]{1,0:T(8,128)S(1)}, f32[5,3328]{1,0:T(8,128)}, u32[]{:S(2)}) copy-start(f32[5,3328]{1,0:T(8,128)} %param.46) | copy-start | bytes 199684
  895.9 180.8 %copy-start.134 = (f32[48,48]{1,0:T(8,128)S(1)}, f32[48,48]{1,0:T(8,128)}, u32[]{:S(2)}) copy-start(f32[48,48]{1,0:T(8,128)} %param.41) | copy-start | bytes 27652
  895.9 180.8 %copy-start.144 = (f32[48,48]{1,0:T(8,128)S(1)}, f32[48,48]{1,0:T(8,128)}, u32[]{:S(2)}) copy-start(f32[48,48]{1,0:T(8,128)} %param.42) | copy-start | bytes 27652
  895.9 180.8 %copy-start.145 = (f32[48,48]{1,0:T(8,128)S(1)}, f32[48,48]{1,0:T(8,128)}, u32[]{:S(2)}) copy-start(f32[48,48]{1,0:T(8,128)} %param.43) | copy-start | bytes 27652
  895.9 215.6 %copy-start.77 = (f32[384,384]{1,0:T(8,128)S(1)}, f32[384,384]{1,0:T(8,128)}, u32[]{:S(2)}) copy-start(f32[384,384]{1,0:T(8,128)} %param.53) | copy-start | bytes 1769476
  895.9 215.6 %copy-start.87 = (f32[384,384]{1,0:T(8,128)S(1)}, f32[384,384]{1,0:T(8,128)}, u32[]{:S(2)}) copy-start(f32[384,384]{1,0:T(8,128)} %param.54) | copy-start | bytes 1769476
  895.9 215.6 %copy-start.88 = (f32[384,384]{1,0:T(8,128)S(1)}, f32[384,384]{1,0:T(8,128)}, u32[]{:S(2)}) copy-start(f32[384,384]{1,0:T(8,128)} %param.55) | copy-start | bytes 1769476
  896.7 217.3 %copy-start.141 = (f32[3072]{0:T(1024)}, f32[3072]{0:T(1024)S(1)}, u32[]{:S(2)}) copy-start(f32[3072]{0:T(1024)S(1)} %dynamic_update_slice.62) | copy-start | bytes 36868
  896.8 179.8 %copy-start.151 = (f32[3,48]{1,0:T(4,128)}, f32[3,48]{1,0:T(4,128)S(1)}, u32[]{:S(2)}) copy-start(f32[3,48]{1,0:T(4,128)S(1)} %dynamic_update_slice.61) | copy-start | bytes 1732
  1078.0 137.2 %copy-start.119 = (f32[48,256]{1,0:T(8,128)S(1)}, f32[48,256]{1,0:T(8,128)}, u32[]{:S(2)}) copy-start(f32[48,256]{1,0:T(8,128)} %param.38) | copy-start | bytes 147460
  1078.0 137.2 %copy-start.142 = (f32[48,256]{1,0:T(8,128)S(1)}, f32[48,256]{1,0:T(8,128)}, u32[]{:S(2)}) copy-start(f32[48,256]{1,0:T(8,128)} %param.39) | copy-start | bytes 147460
  1078.0 137.2 %copy-start.143 = (f32[48,256]{1,0:T(8,128)S(1)}, f32[48,256]{1,0:T(8,128)}, u32[]{:S(2)}) copy-start(f32[48,256]{1,0:T(8,128)} %param.40) | copy-start | bytes 147460
  1078.0 187.2 %copy-start.67 = (f32[384,768]{1,0:T(8,128)S(1)}, f32[384,768]{1,0:T(8,128)}, u32[]{:S(2)}) copy-start(f32[384,768]{1,0:T(8,128)} %param.35) | copy-start | bytes 3538948
  1216.7 259.6 %copy-start.63 = (bf16[1536,256]{1,0:T(8,128)(2,1)S(1)}, bf16[1536,256]{1,0:T(8,128)(2,1)}, u32[]{:S(2)}) copy-start(bf16[1536,256]{1,0:T(8,128)(2,1)} %copy-done.62) | copy-start | bytes 2359300
  1216.7 259.6 %copy-start.84 = (f32[256,256]{1,0:T(8,128)S(1)}, f32[256,256]{1,0:T(8,128)}, u32[]{:S(2)}) copy-start(f32[256,256]{1,0:T(8,128)} %reduce-scatter.13.cloned.1.call-done) | copy-start | bytes 786436
  1269.6 208.6 %copy-start.52 = (bf16[256,1536]{1,0:T(8,128)(2,1)S(1)}, bf16[256,1536]{1,0:T(8,128)(2,1)}, u32[]{:S(2)}) copy-start(bf16[256,1536]{1,0:T(8,128)(2,1)} %param.30) | copy-start | bytes 2359300
  1269.6 208.6 %copy-start.69 = (bf16[1536,48]{1,0:T(8,128)(2,1)S(1)}, bf16[1536,48]{1,0:T(8,128)(2,1)}, u32[]{:S(2)}) copy-start(bf16[1536,48]{1,0:T(8,128)(2,1)} %copy-done.68) | copy-start | bytes 442372
  1269.6 208.6 %copy-start.124 = (f32[1536]{0:T(1024)S(1)}, f32[1536]{0:T(1024)}, u32[]{:S(2)}) copy-start(f32[1536]{0:T(1024)} %param.32) | copy-start | bytes 18436
  1478.2 209.1 %copy-start.72 = (bf16[256,1536]{1,0:T(8,128)(2,1)S(1)}, bf16[256,1536]{1,0:T(8,128)(2,1)}, u32[]{:S(2)}) copy-start(bf16[256,1536]{1,0:T(8,128)(2,1)} %param.31) | copy-start | bytes 2359300
  1523.0 167.8 %copy-start.148 = (f32[3072]{0:T(1024)}, f32[3072]{0:T(1024)S(1)}, u32[]{:S(2)}) copy-start(f32[3072]{0:T(1024)S(1)} %get-tuple-element.1836) | copy-start | bytes 36868
  1523.0 167.8 %copy-start.149 = (f32[1536]{0:T(1024)}, f32[1536]{0:T(1024)S(1)}, u32[]{:S(2)}) copy-start(f32[1536]{0:T(1024)S(1)} %get-tuple-element.1830) | copy-start | bytes 18436
  1523.0 167.8 %copy-start.152 = (f32[3,48]{1,0:T(4,128)}, f32[3,48]{1,0:T(4,128)S(1)}, u32[]{:S(2)}) copy-start(f32[3,48]{1,0:T(4,128)S(1)} %get-tuple-element.1835) | copy-start | bytes 1732
  (208 other events, 577.6 us)
Sparse Core Ops, SparseCore 0:
  88.8 38.3 all-gather.9
  129.3 23.3 all-gather.7
  155.3 102.3 all-gather.5
  259.7 15.6 all-gather.11
  277.3 99.5 all-gather.13
  712.3 62.5 reduce-scatter.14
  778.4 67.5 reduce-scatter.12
  852.1 121.6 all-reduce.37
  979.5 97.1 reduce-scatter.20
  1079.6 31.8 reduce-scatter.22
  1117.3 97.9 reduce-scatter.18
  1218.2 47.0 reduce-scatter.16
  1268.9 207.4 reduce-scatter.10
  1479.8 207.4 reduce-scatter.8
where the time goes:
time: 1710 us; the launch traced here: 1700 us
  waiting for transfers between devices  908 us (53%)
  blocking collectives  260 us (15%)
  other arithmetic  195 us (11%)
  matrix products  170 us (10%)
  local copies, waits for them, and re-layouts  138 us (8%)
    reduce_scatter x1, waiting for transfers between devices, per_device(): lax.psum_scatter(jnp.einsum('tc,dc->td', rows, in_local, preferred_elemen...  207 us
    reduce_scatter x1, waiting for transfers between devices, per_device(): lax.psum_scatter(jnp.dot(rows, out_local, preferred_element_type=jnp.floa...  160 us
    reduce_scatter x1, waiting for transfers between devices, per_device(): lax.psum_scatter(grad_state_part, ('dp', 'row', 'col'), scatter_dimension...  101 us
    reduce_scatter x1, waiting for transfers between devices, per_device(): lax.psum_scatter(grad_step_part, ('dp', 'row', 'col'), scatter_dimension=...  101 us
    another operation x25, other arithmetic  91 us
    all_gather x1, blocking collectives, per_device(): lax.all_gather(state_proj.astype(jnp.bfloat16), ('dp', 'row', 'col'), axi...  77.2 us
    psum x1, waiting for transfers between devices, per_device(): lax.psum((norm_part, gated_spread, conv_spread, coef_spread), ('dp', 'row...  76.9 us
    all_gather x1, blocking collectives, per_device(): lax.all_gather(step_proj.astype(jnp.bfloat16), ('dp', 'row', 'col'), axis...  68.2 us
  transfers between devices with their start and end apart: 14, of which 10 were waited for; matrix products, arithmetic and copies ran while one was open for 10% of the time, Pallas kernels for 0%

commit v1 on v0

--- a/solution.py
+++ b/solution.py
@@ -14,6 +14,28 @@
 MATRIX_RATE = 0.003
 VECTOR_RATE = 0.1
 WEIGHT_DECAY = 0.1
+
+
+def in_order(blocks, dim):
+    blocks = jnp.moveaxis(blocks, 0, dim)
+    shape = blocks.shape
+    return blocks.reshape(*shape[:dim], shape[dim] * shape[dim + 1], *shape[dim + 2 :])
+
+
+def collect(shard, axis, dim):
+    size = lax.axis_size(axis)
+    pairs = [(i, (i + 1) % size) for i in range(size)]
+    back = [(b, a) for a, b in pairs]
+    lower, upper = ([], [])
+    for lap in range(size - 1):
+        if lap % 2 == 0:
+            lower.append(lax.ppermute(lower[-1] if lower else shard, axis, pairs))
+        else:
+            upper.append(lax.ppermute(upper[-1] if upper else shard, axis, back))
+    pieces = jnp.stack([*lower[::-1], shard, *upper])
+    shift = lax.axis_index(axis) - len(lower)
+    pieces = pieces[(jnp.arange(size) - shift) % size]
+    return in_order(pieces, dim)
 
 
 def causal_conv(values, filters):
@@ -157,7 +179,7 @@
         jnp.bfloat16
     )
     normed_all, state_all, step_all, cotangent = (
-        lax.all_gather(normed_in, ("row", "col"), axis=0, tiled=True),
+        collect(normed_in, ("row", "col"), 0),
         lax.all_gather(state_own, ("row", "col"), axis=0, tiled=True),
         lax.all_gather(step_own, ("row", "col"), axis=0, tiled=True),
         lax.all_gather(out_grad, ("row", "col"), axis=0, tiled=True),

time: 1710 us -> 1900 us (1.11)
  local copies, waits for them, and re-layouts: 138 us -> 219 us
  blocking collectives: 260 us -> 313 us
  waiting for transfers between devices: 908 us -> 943 us
    ppermute x0 -> x7, waiting for transfers between devices: none -> 80.8 us  [the longest x3 50.8 us: collect(): upper.append(lax.ppermute(upper[-1] if upper else shard, axis, back))]
    dynamic_update_slice x0 -> x8, local copies, waits for them, and re-layouts: none -> 77.9 us  [mixer_all(): lax.map(jax.checkpoint(sequence), (gate_part.reshape(seq_count, SEQ_LEN,...]
    all_gather x1 -> x0, waiting for transfers between devices: 55.3 us -> none  [per_device(): lax.all_gather(normed_in, ('row', 'col'), axis=0, tiled=True)]
    all_gather x1, blocking collectives: 68.2 us -> 102 us  [per_device(): lax.all_gather(step_proj.astype(jnp.bfloat16), ('dp', 'row', 'col'), axis...]
    all_gather x1, blocking collectives: 32.7 us -> 53.2 us  [per_device(): lax.all_gather(step_own, ('row', 'col'), axis=0, tiled=True)]
    another operation x26 -> x25, other arithmetic: 93.2 us -> 91 us
  transfers between devices with their start and end apart: 14 -> 20, of which waited for: 10 -> 13; matrix products, arithmetic and copies ran while one was open for 10% -> 10% of each run, Pallas kernels for 0% -> 0%
where the time goes in v1:
time: 1900 us; the launch traced here: 1880 us
  waiting for transfers between devices  943 us (50%)
  blocking collectives  313 us (16%)
  local copies, waits for them, and re-layouts  219 us (12%)
  other arithmetic  205 us (11%)
  matrix products  168 us (9%)
    reduce_scatter x1, waiting for transfers between devices, per_device(): lax.psum_scatter(jnp.einsum('tc,dc->td', rows, in_local, preferred_elemen...  207 us
    reduce_scatter x1, waiting for transfers between devices, per_device(): lax.psum_scatter(jnp.dot(rows, out_local, preferred_element_type=jnp.floa...  160 us
    all_gather x1, blocking collectives, per_device(): lax.all_gather(step_proj.astype(jnp.bfloat16), ('dp', 'row', 'col'), axis...  102 us
    reduce_scatter x1, waiting for transfers between devices, per_device(): lax.psum_scatter(grad_step_part, ('dp', 'row', 'col'), scatter_dimension=...  102 us
    reduce_scatter x1, waiting for transfers between devices, per_device(): lax.psum_scatter(grad_state_part, ('dp', 'row', 'col'), scatter_dimension...  101 us
    another operation x25, other arithmetic  91 us
    psum x1, waiting for transfers between devices, per_device(): lax.psum((norm_part, gated_spread, conv_spread, coef_spread), ('dp', 'row...  86.8 us
    dynamic_update_slice x8, local copies, waits for them, and re-layouts, mixer_all(): lax.map(jax.checkpoint(sequence), (gate_part.reshape(seq_count, SEQ_LEN,...  77.9 us
  transfers between devices with their start and end apart: 20, of which 13 were waited for; matrix products, arithmetic and copies ran while one was open for 10% of the time, Pallas kernels for 0%

profile of v1, /device:TPU:0, one launch (start us, length us, event | category | flops | bytes accessed | tf_op | source)
XLA Modules:
  0.0 1881.8 jit_solution(12936906484736239113)
XLA Ops:
  10.1 77.2 %all_gather.22 = bf16[1536,256]{1,0:T(8,128)(2,1)S(1)} all-gather(bf16[48,256]{1,0:T(8,128)(2,1)S(1)} %convert_element_type.67), channel_id=1, replica_groups=mesh['dp'=4,'row'=2,'col'=4] {'dp','row','col'}, dimensions={0}, use_global_device_ids=true | all-gather | bytes 811008 | tf_op jit(solution)/shard_map/all_gather | solution.py:169
  91.2 21.5 %collective-permute-done = bf16[256,1536]{1,0:T(8,128)(2,1)S(1)} collective-permute-done((bf16[256,1536]{1,0:T(8,128)(2,1)S(1)}, bf16[256,1536]{1,0:T(8,128)(2,1)S(1)}, u32[]{:S(2)}, u32[]{:S(2)}) %collective-permute-start) | collective-permute-done | bytes 786464 | tf_op jit(solution)/shard_map/ppermute | solution.py:32
  112.7 4.7 collective-permute-start.4
  117.6 102.2 %all_gather.24 = bf16[1536,48]{1,0:T(8,128)(2,1)S(1)} all-gather(bf16[48,48]{1,0:T(8,128)(2,1)S(1)} %convert_element_type.69), channel_id=1, replica_groups=mesh['dp'=4,'row'=2,'col'=4] {'dp','row','col'}, dimensions={0}, use_global_device_ids=true | all-gather | bytes 152064 | tf_op jit(solution)/shard_map/all_gather | solution.py:170
  220.1 53.2 %all_gather.25 = bf16[2048,48]{0,1:T(8,128)(2,1)S(1)} all-gather(bf16[256,48]{0,1:T(8,128)(2,1)S(1)} %convolution_convert_fusion.1), channel_id=1, replica_groups=mesh['dp'=4,'row'=2,'col'=4] {'row','col'}, dimensions={0}, use_global_device_ids=true | all-gather | bytes 221184 | tf_op jit(solution)/shard_map/all_gather | solution.py:184
  278.3 47.7 %collective-permute-done.5 = bf16[256,1536]{1,0:T(8,128)(2,1)S(1)} collective-permute-done((bf16[256,1536]{1,0:T(8,128)(2,1)S(1)}, bf16[256,1536]{1,0:T(8,128)(2,1)S(1)}, u32[]{:S(2)}, u32[]{:S(2)}) %collective-permute-start.5) | collective-permute-done | bytes 786464 | tf_op jit(solution)/shard_map/ppermute | solution.py:34
  328.7 8.5 collective-permute-done.3
  347.4 3.1 collective-permute-done.6
  352.7 6.4 gather_fusion
  361.9 7.2 fusion.182
  372.2 4.2 reshape_reshape_squeeze.7
  379.1 4.2 reshape_reshape_squeeze.6
  386.0 81.4 %while.41 = (s32[]{:T(128)}, f32[2,1024,384]{1,2,0:T(8,128)}, f32[1,384]{1,0:T(1,128)}, f32[2,1024,384]{1,2,0:T(8,128)}, f32[1,384]{1,0:T(1,128)}, /*index=5*/f3...) while((s32[]{:T(128)}, f32[2,1024,384]{1,2,0:T(8,128)}, ...), condition=%wide.region_4.5_spmd.clone, body=%wide.region_1.4_spmd.clone.sunk | while | flops 2843105280 | bytes 111482184 | solution.py:106
  388.7 7.2 reduce-window.78
  412.6 7.2 bitcast_add_fusion.11
  429.1 7.2 reduce-window.78
  453.0 7.2 bitcast_add_fusion.11
  467.4 3.7 copy.353
  471.5 19.4 %psum.42 = f32[2048]{0:T(1024)S(1)} all-reduce(f32[2048]{0:T(1024)S(1)} %bitcast.657), channel_id=1, replica_groups=mesh['dp'=4,'row'=2,'col'=4] {'row','col'}, use_global_device_ids=true, to_apply=%region_6.7 | all-reduce | flops 2048 | bytes 16384 | tf_op jit(solution)/shard_map/psum | solution.py:207
  490.9 10.1 fusion.136
  501.0 17.7 psum.43
  518.8 4.1 fusion.133
  529.0 364.1 %while.42 = (s32[]{:T(128)}, f32[5,384]{1,0:T(8,128)}, f32[5,256]{1,0:T(8,128)}, f32[3,6]{1,0:T(4,128)}, bf16[2,1024,384]{1,0,2:T(2,128)(2,1)}, /*index=5*/bf16[...) while((s32[]{:T(128)}, f32[5,384]{1,0:T(8,128)}, ...), condition=%wide.region_38.39_spmd.clone, body=%wide.region_10.38_spmd.clone.sunk | while | flops 8533547008 | bytes 279750528 | solution.py:106
  534.7 4.6 dynamic-slice_bitcast_fusion.13
  541.5 7.2 reduce-window.81
  553.4 4.2 fusion.317
  562.1 5.6 bitcast_add_fusion.12
  570.3 3.2 broadcast_multiply_fusion.17
  580.4 3.5 fusion.324
  592.3 3.8 fusion.327
  599.6 9.0 bitcast_add_fusion.13
  608.6 9.6 fusion.325
  623.2 30.3 %reduce-window.82 = f32[4,6,2,128]{3,2,1,0:T(2,128)S(1)} reduce-window(f32[4,6,2,128]{3,2,1,0:T(2,128)S(1)} %reshape.814, f32[]{:T(128)} %constant.278.clone.1..sunk.1), window={size=1x1x1x128 pad=0_0x0_0x0_0x0_127}, to_apply=%region_33.33 | reduce-window | flops 780288 | bytes 49156 | tf_op jit(solution)/shard_map/reduce-window.36
  660.5 26.0 %dynamic_update_slice.80 = bf16[2,1024,384]{1,0,2:T(2,128)(2,1)} dynamic-update-slice(bf16[2,1024,384]{1,0,2:T(2,128)(2,1)} %get-tuple-element.1669, bf16[1,1024,384]{1,0,2:T(2,128)(2,1)S(1)} %copy.526, s32[]{:T(128)S(6)} %sub.399, s32[]{:T(128)} %constant.277.clone.1..sunk, s32[]{:T(128)} %constant.277.clone.1..sunk) | dynamic-update-slice | bytes 1572868 | tf_op jit(solution)/shard_map/transpose(jvp())/while/body/jit(dynamic_update_index_in_dim)/dynamic_update_slice | solution.py:106
  695.6 10.5 dynamic_update_slice.81
  713.3 4.6 dynamic-slice_bitcast_fusion.13
  720.1 7.2 reduce-window.81
  732.0 4.2 fusion.317
  740.7 5.6 bitcast_add_fusion.12
  748.8 3.2 broadcast_multiply_fusion.17
  759.0 3.5 fusion.324
  770.8 3.8 fusion.327
  778.2 8.8 bitcast_add_fusion.13
  787.0 9.6 fusion.325
  801.5 30.6 %reduce-window.82 = f32[4,6,2,128]{3,2,1,0:T(2,128)S(1)} reduce-window(f32[4,6,2,128]{3,2,1,0:T(2,128)S(1)} %reshape.814, f32[]{:T(128)} %constant.278.clone.1..sunk.1), window={size=1x1x1x128 pad=0_0x0_0x0_0x0_127}, to_apply=%region_33.33 | reduce-window | flops 780288 | bytes 49156 | tf_op jit(solution)/shard_map/reduce-window.36
  839.1 26.0 %dynamic_update_slice.80 = bf16[2,1024,384]{1,0,2:T(2,128)(2,1)} dynamic-update-slice(bf16[2,1024,384]{1,0,2:T(2,128)(2,1)} %get-tuple-element.1669, bf16[1,1024,384]{1,0,2:T(2,128)(2,1)S(1)} %copy.526, s32[]{:T(128)S(6)} %sub.399, s32[]{:T(128)} %constant.277.clone.1..sunk, s32[]{:T(128)} %constant.277.clone.1..sunk) | dynamic-update-slice | bytes 1572868 | tf_op jit(solution)/shard_map/transpose(jvp())/while/body/jit(dynamic_update_index_in_dim)/dynamic_update_slice | solution.py:106
  874.2 10.5 dynamic_update_slice.81
  896.5 61.4 %reduce-scatter.15.cloned.1.call-done = f32[256,48]{0,1:T(8,128)} async-done(((f32[2048,48]{0,1:T(8,128)}), f32[256,48]{0,1:T(8,128)}) %reduce-scatter.15.cloned.1.call-update) | async-done | bytes 49168 | tf_op jit(solution)/shard_map/reduce_scatter | solution.py:254
  960.1 6.8 fusion.186
  967.0 61.7 %reduce-scatter.13.cloned.1.call-done = f32[256,256]{1,0:T(8,128)} async-done(((f32[2048,256]{1,0:T(8,128)}), f32[256,256]{1,0:T(8,128)}) %reduce-scatter.13.cloned.1.call-update) | async-done | bytes 262160 | tf_op jit(solution)/shard_map/reduce_scatter | solution.py:253
  1031.3 4.0 reshape.710
  1041.9 8.7 fusion.185
  1050.7 10.1 fusion.184
  1062.1 6.6 fusion.183
  1069.8 86.8 %all-reduce.38.cloned.1.call-done = f32[5,3328]{1,0:T(8,128)} async-done(((f32[5,3328]{1,0:T(8,128)}), f32[5,3328]{1,0:T(8,128)}) %all-reduce.38.cloned.1.call-update) | async-done | bytes 66576 | tf_op jit(solution)/shard_map/psum | solution.py:294
  1158.3 101.7 %reduce-scatter.21.cloned.1.call-done = f32[48,48]{1,0:T(8,128)} async-done(((f32[1536,48]{1,0:T(8,128)}), f32[48,48]{1,0:T(8,128)}) %reduce-scatter.21.cloned.1.call-update) | async-done | bytes 9232 | tf_op jit(solution)/shard_map/reduce_scatter | solution.py:271
  1261.4 33.6 %reduce-scatter.23.cloned.1.call-done = f32[384,384]{1,0:T(8,128)} async-done(((f32[384,1536]{1,0:T(8,128)}), f32[384,384]{1,0:T(8,128)}) %reduce-scatter.23.cloned.1.call-update) | async-done | bytes 589840 | tf_op jit(solution)/shard_map/reduce_scatter | solution.py:275
  1297.5 101.1 %reduce-scatter.19.cloned.1.call-done = f32[48,256]{1,0:T(8,128)} async-done(((f32[1536,256]{1,0:T(8,128)}), f32[48,256]{1,0:T(8,128)}) %reduce-scatter.19.cloned.1.call-update) | async-done | bytes 49168 | tf_op jit(solution)/shard_map/reduce_scatter | solution.py:270
  1400.1 48.7 %reduce-scatter.17.cloned.1.call-done = f32[384,768]{1,0:T(8,128)} async-done(((f32[1536,768]{1,0:T(8,128)}), f32[384,768]{1,0:T(8,128)}) %reduce-scatter.17.cloned.1.call-update) | async-done | bytes 1179664 | tf_op jit(solution)/shard_map/reduce_scatter | solution.py:274
  1448.8 4.3 multiply_subtract_fusion
  1453.2 206.6 %reduce-scatter.11.cloned.1.call-done = f32[256,1536]{1,0:T(8,128)} async-done(((f32[2048,1536]{1,0:T(8,128)}), f32[256,1536]{1,0:T(8,128)}) %reduce-scatter.11.cloned.1.call-update) | async-done | bytes 1572880 | tf_op jit(solution)/shard_map/reduce_scatter | solution.py:243
  1662.9 43.5 %all-reduce.35 = (f32[1536]{0:T(1024)S(1)}, f32[3,48]{1,0:T(4,128)S(1)}, f32[3072]{0:T(1024)S(1)}) all-reduce(f32[1536]{0:T(1024)S(1)} %get-tuple-element.1000, f32[3,48]{1,0:T(4,128)} %copy-done.151, f32[3072]{0:T(1024)} %copy-done.136), channel_id=1, replica_groups=mesh['dp'=4,'row'=2,'col'=4] {'dp','row','col'}, use_global_device_ids=true, to_apply=%region_44.45 | all-reduce | flops 4752 | bytes 38016 | tf_op jit(solution)/shard_map/psum | solution.py:294
  1711.2 159.6 %reduce-scatter.9.cloned.1.call-done = f32[256,1536]{1,0:T(8,128)} async-done(((f32[2048,1536]{1,0:T(8,128)}), f32[256,1536]{1,0:T(8,128)}) %reduce-scatter.9.cloned.1.call-update) | async-done | bytes 1572880 | tf_op jit(solution)/shard_map/reduce_scatter | solution.py:212
  1870.8 3.4 fusion.142
  (883 shorter events, 247.4 us)
Async XLA Ops:
  7.2 80.1 %copy-start.43 = (bf16[256,1536]{1,0:T(8,128)(2,1)S(1)}, bf16[256,1536]{1,0:T(8,128)(2,1)}, u32[]{:S(2)}) copy-start(bf16[256,1536]{1,0:T(8,128)(2,1)} %param.30) | copy-start | bytes 2359300
  7.2 80.1 %copy-start.110 = (f32[1536]{0:T(1024)S(1)}, f32[1536]{0:T(1024)}, u32[]{:S(2)}) copy-start(f32[1536]{0:T(1024)} %param.32) | copy-start | bytes 18436
  7.2 318.7 %all-gather.7.cloned.1.call-start = ((), (), s32[]{:S(2)}) async-start(), calls=%async_computation.9 | async-start | bytes 1179648 | tf_op jit(solution)/shard_map/all_gather | solution.py:183
  9.3 335.0 %copy-start.140 = (f32[256]{0:T(256)}, f32[256]{0:T(256)S(1)}, u32[]{:S(2)}) copy-start(f32[256]{0:T(256)S(1)} %get-tuple-element.1186) | copy-start | bytes 3076
  88.2 131.6 %copy-start.41 = (bf16[256,1536]{1,0:T(8,128)(2,1)}, bf16[256,1536]{1,0:T(8,128)(2,1)S(1)}, u32[]{:S(2)}) copy-start(bf16[256,1536]{1,0:T(8,128)(2,1)S(1)} %fusion.139) | copy-start | bytes 2359300
  89.2 269.8 %all-gather.5.cloned.1.call-start = ((), (), s32[]{:S(2)}) async-start(), calls=%async_computation.8 | async-start | bytes 2949120 | tf_op jit(solution)/shard_map/all_gather | solution.py:165
  90.2 27.4 %copy-start.128 = (f32[48,48]{1,0:T(8,128)S(1)}, f32[48,48]{1,0:T(8,128)}, u32[]{:S(2)}) copy-start(f32[48,48]{1,0:T(8,128)} %param.41) | copy-start | bytes 27652
  90.2 400.7 %all-gather.9.cloned.1.call-start = ((), (), s32[]{:S(2)}) async-start(), calls=%async_computation.10 | async-start | bytes 1474560 | tf_op jit(solution)/shard_map/all_gather | solution.py:166
  91.1 183.7 %copy-start.116 = (f32[5,3328]{1,0:T(8,128)S(1)}, f32[5,3328]{1,0:T(8,128)}, u32[]{:S(2)}) copy-start(f32[5,3328]{1,0:T(8,128)} %param.44) | copy-start | bytes 199684
  91.1 186.5 %copy-start.150 = (f32[3,48]{1,0:T(4,128)S(1)}, f32[3,48]{1,0:T(4,128)}, u32[]{:S(2)}) copy-start(f32[3,48]{1,0:T(4,128)} %param.47) | copy-start | bytes 1732
  91.1 399.8 %all-gather.11.cloned.1.call-start = ((), (), s32[]{:S(2)}) async-start(), calls=%async_computation.12 | async-start | bytes 7077888 | tf_op jit(solution)/shard_map/all_gather | solution.py:185
  91.1 21.6 %collective-permute-start = (bf16[256,1536]{1,0:T(8,128)(2,1)S(1)}, bf16[256,1536]{1,0:T(8,128)(2,1)S(1)}, u32[]{:S(2)}, u32[]{:S(2)}) collective-permute-start(bf16[256,1536]{1,0:T(8,128)(2,1)S(1)} %fusion.139), channel_id=1, source_target_pairs={{0,1},{1,2},{2,3},{3,4},{4,5},{5,6},{6,7},{7,0},{8,9},{9,10},{10,1... | collective-permute-start | bytes 2359304 | tf_op jit(solution)/shard_map/ppermute | solution.py:32
  112.7 107.0 %collective-permute-start.1 = (bf16[256,1536]{1,0:T(8,128)(2,1)S(1)}, bf16[256,1536]{1,0:T(8,128)(2,1)}, u32[]{:S(2)}, u32[]{:S(2)}) collective-permute-start(bf16[256,1536]{1,0:T(8,128)(2,1)S(1)} %collective-permute-done), channel_id=1, source_target_pairs={{0,1},{1,2},{2,3},{3,4},{4,5},{5,6},{6,7},{7,0},{8,9},{9,10},{10,1... | collective-permute-start | bytes 2359304 | tf_op jit(solution)/shard_map/ppermute | solution.py:32
  112.7 162.8 %collective-permute-start.4 = (bf16[256,1536]{1,0:T(8,128)(2,1)S(1)}, bf16[256,1536]{1,0:T(8,128)(2,1)S(1)}, u32[]{:S(2)}, u32[]{:S(2)}) collective-permute-start(bf16[256,1536]{1,0:T(8,128)(2,1)S(1)} %fusion.139), channel_id=1, source_target_pairs={{1,0},{2,1},{3,2},{4,3},{5,4},{6,5},{7,6},{0,7},{9,8},{10,9},{11,1... | collective-permute-start | bytes 2359304 | tf_op jit(solution)/shard_map/ppermute | solution.py:34
  117.5 840.5 %reduce-scatter.15.cloned.1.call-start = ((), (), s32[]{:S(2)}) async-start(), calls=%async_computation.15 | async-start | bytes 442368 | tf_op jit(solution)/shard_map/reduce_scatter | solution.py:254
  219.7 55.7 %copy-start.62 = (bf16[1536,48]{1,0:T(8,128)(2,1)}, bf16[1536,48]{1,0:T(8,128)(2,1)S(1)}, u32[]{:S(2)}) copy-start(bf16[1536,48]{1,0:T(8,128)(2,1)S(1)} %all_gather.24) | copy-start | bytes 442372
  219.8 57.2 %collective-permute-start.2 = (bf16[256,1536]{1,0:T(8,128)(2,1)}, bf16[256,1536]{1,0:T(8,128)(2,1)}, u32[]{:S(2)}, u32[]{:S(2)}) collective-permute-start(bf16[256,1536]{1,0:T(8,128)(2,1)} %collective-permute-done.1), channel_id=1, source_target_pairs={{0,1},{1,2},{2,3},{3,4},{4,5},{5,6},{6,7},{7,0},{8,9},{9,10},{10,1... | collective-permute-start | bytes 2359304 | tf_op jit(solution)/shard_map/ppermute | solution.py:32
  275.5 50.5 %collective-permute-start.5 = (bf16[256,1536]{1,0:T(8,128)(2,1)S(1)}, bf16[256,1536]{1,0:T(8,128)(2,1)S(1)}, u32[]{:S(2)}, u32[]{:S(2)}) collective-permute-start(bf16[256,1536]{1,0:T(8,128)(2,1)S(1)} %collective-permute-done.4), channel_id=1, source_target_pairs={{1,0},{2,1},{3,2},{4,3},{5,4},{6,5},{7,6},{0,7},{9,8},{10,9},{11,1... | collective-permute-start | bytes 2359304 | tf_op jit(solution)/shard_map/ppermute | solution.py:34
  276.9 60.3 %collective-permute-start.3 = (bf16[256,1536]{1,0:T(8,128)(2,1)}, bf16[256,1536]{1,0:T(8,128)(2,1)}, u32[]{:S(2)}, u32[]{:S(2)}) collective-permute-start(bf16[256,1536]{1,0:T(8,128)(2,1)} %collective-permute-done.2), channel_id=1, source_target_pairs={{0,1},{1,2},{2,3},{3,4},{4,5},{5,6},{6,7},{7,0},{8,9},{9,10},{10,1... | collective-permute-start | bytes 2359304 | tf_op jit(solution)/shard_map/ppermute | solution.py:32
  325.9 24.6 %collective-permute-start.6 = (bf16[256,1536]{1,0:T(8,128)(2,1)S(1)}, bf16[256,1536]{1,0:T(8,128)(2,1)}, u32[]{:S(2)}, u32[]{:S(2)}) collective-permute-start(bf16[256,1536]{1,0:T(8,128)(2,1)S(1)} %collective-permute-done.5), channel_id=1, source_target_pairs={{1,0},{2,1},{3,2},{4,3},{5,4},{6,5},{7,6},{0,7},{9,8},{10,9},{11,1... | collective-permute-start | bytes 2359304 | tf_op jit(solution)/shard_map/ppermute | solution.py:34
  490.9 27.8 %copy-start.48 = (f32[2,1024,384]{2,1,0:T(8,128)S(1)}, f32[2,1024,384]{2,1,0:T(8,128)}, u32[]{:S(2)}) copy-start(f32[2,1024,384]{2,1,0:T(8,128)} %copy.353) | copy-start | bytes 9437188
  621.3 32.2 %copy-start.31 = (f32[4,256,6,64]{1,3,2,0:T(8,128)S(1)}, f32[4,256,6,64]{1,3,2,0:T(8,128)}, u32[]{:S(2)}) copy-start(f32[4,256,6,64]{1,3,2,0:T(8,128)} %bitcast_add_fusion.13) | copy-start | bytes 4718596 | tf_op jit(solution)/shard_map/transpose(jvp())/while
  659.1 27.4 %copy-start.93 = (f32[2,1024,6]{1,2,0:T(8,128)}, f32[2,1024,6]{1,2,0:T(8,128)S(1)}, u32[]{:S(2)}) copy-start(f32[2,1024,6]{1,2,0:T(8,128)S(1)} %get-tuple-element.1692) | copy-start | bytes 147460 | tf_op jit(solution)/shard_map/transpose(jvp())/while
  659.3 27.3 %copy-start.131 = (f32[3,6]{1,0:T(4,128)}, f32[3,6]{1,0:T(4,128)S(1)}, u32[]{:S(2)}) copy-start(f32[3,6]{1,0:T(4,128)S(1)} %select_add_fusion.8) | copy-start | bytes 220 | tf_op jit(solution)/shard_map/transpose(jvp())/while
  660.5 26.0 %copy-start.11 = (f32[1024,256]{1,0:T(8,128)S(1)}, f32[1024,256]{1,0:T(8,128)}, u32[]{:S(2)}) copy-start(f32[1024,256]{1,0:T(8,128)} %dynamic-slice_bitcast_fusion.14) | copy-start | bytes 3145732 | tf_op jit(solution)/shard_map/transpose(jvp())/while
  799.6 32.5 %copy-start.31 = (f32[4,256,6,64]{1,3,2,0:T(8,128)S(1)}, f32[4,256,6,64]{1,3,2,0:T(8,128)}, u32[]{:S(2)}) copy-start(f32[4,256,6,64]{1,3,2,0:T(8,128)} %bitcast_add_fusion.13) | copy-start | bytes 4718596 | tf_op jit(solution)/shard_map/transpose(jvp())/while
  837.7 27.4 %copy-start.93 = (f32[2,1024,6]{1,2,0:T(8,128)}, f32[2,1024,6]{1,2,0:T(8,128)S(1)}, u32[]{:S(2)}) copy-start(f32[2,1024,6]{1,2,0:T(8,128)S(1)} %get-tuple-element.1692) | copy-start | bytes 147460 | tf_op jit(solution)/shard_map/transpose(jvp())/while
  837.9 27.3 %copy-start.131 = (f32[3,6]{1,0:T(4,128)}, f32[3,6]{1,0:T(4,128)S(1)}, u32[]{:S(2)}) copy-start(f32[3,6]{1,0:T(4,128)S(1)} %select_add_fusion.8) | copy-start | bytes 220 | tf_op jit(solution)/shard_map/transpose(jvp())/while
  839.1 26.0 %copy-start.11 = (f32[1024,256]{1,0:T(8,128)S(1)}, f32[1024,256]{1,0:T(8,128)}, u32[]{:S(2)}) copy-start(f32[1024,256]{1,0:T(8,128)} %dynamic-slice_bitcast_fusion.14) | copy-start | bytes 3145732 | tf_op jit(solution)/shard_map/transpose(jvp())/while
  839.1 26.0 %copy-start.95 = (f32[1,256]{1,0:T(1,128)S(1)}, f32[1,256]{1,0:T(1,128)}, u32[]{:S(2)}) copy-start(f32[1,256]{1,0:T(1,128)} %copy-done.94) | copy-start | bytes 3076 | tf_op jit(solution)/shard_map/transpose(jvp())/while
  893.1 64.9 %copy-start.42 = (bf16[256,1536]{1,0:T(8,128)(2,1)S(1)}, bf16[256,1536]{1,0:T(8,128)(2,1)}, u32[]{:S(2)}) copy-start(bf16[256,1536]{1,0:T(8,128)(2,1)} %copy-done.41) | copy-start | bytes 2359300
  895.1 133.6 %reduce-scatter.13.cloned.1.call-start = ((), (), s32[]{:S(2)}) async-start(), calls=%async_computation.14 | async-start | bytes 2359296 | tf_op jit(solution)/shard_map/reduce_scatter | solution.py:253
  895.7 64.5 %copy-start.39 = (bf16[2048,384]{1,0:T(8,128)(2,1)S(1)}, bf16[2048,384]{1,0:T(8,128)(2,1)}, u32[]{:S(2)}) copy-start(bf16[2048,384]{1,0:T(8,128)(2,1)} %get-tuple-element.1167) | copy-start | bytes 4718596
  895.7 260.9 %all-reduce.38.cloned.1.call-start = ((), (), s32[]{:S(2)}) async-start(), calls=%async_computation.19 | async-start | bytes 212992 | tf_op jit(solution)/shard_map/psum | solution.py:294
  896.5 363.5 %reduce-scatter.21.cloned.1.call-start = ((), (), s32[]{:S(2)}) async-start(), calls=%async_computation.18 | async-start | bytes 811008 | tf_op jit(solution)/shard_map/reduce_scatter | solution.py:271
  960.1 334.9 %reduce-scatter.23.cloned.1.call-start = ((), (), s32[]{:S(2)}) async-start(), calls=%async_computation.20 | async-start | bytes 2949120 | tf_op jit(solution)/shard_map/reduce_scatter | solution.py:275
  967.0 431.7 %reduce-scatter.19.cloned.1.call-start = ((), (), s32[]{:S(2)}) async-start(), calls=%async_computation.17 | async-start | bytes 1622016 | tf_op jit(solution)/shard_map/reduce_scatter | solution.py:270
  1031.3 417.6 %reduce-scatter.17.cloned.1.call-start = ((), (), s32[]{:S(2)}) async-start(), calls=%async_computation.16 | async-start | bytes 5898240 | tf_op jit(solution)/shard_map/reduce_scatter | solution.py:274
  1050.7 609.1 %reduce-scatter.11.cloned.1.call-start = ((), (), s32[]{:S(2)}) async-start(), calls=%async_computation.13 | async-start | bytes 14155776 | tf_op jit(solution)/shard_map/reduce_scatter | solution.py:243
  1060.9 809.9 %reduce-scatter.9.cloned.1.call-start = ((), (), s32[]{:S(2)}) async-start(), calls=%async_computation.11 | async-start | bytes 14155776 | tf_op jit(solution)/shard_map/reduce_scatter | solution.py:212
  1068.7 87.9 %copy-start.117 = (f32[5,3328]{1,0:T(8,128)S(1)}, f32[5,3328]{1,0:T(8,128)}, u32[]{:S(2)}) copy-start(f32[5,3328]{1,0:T(8,128)} %param.44) | copy-start | bytes 199684
  1068.7 87.9 %copy-start.126 = (f32[5,3328]{1,0:T(8,128)S(1)}, f32[5,3328]{1,0:T(8,128)}, u32[]{:S(2)}) copy-start(f32[5,3328]{1,0:T(8,128)} %param.45) | copy-start | bytes 199684
  1068.7 87.9 %copy-start.127 = (f32[5,3328]{1,0:T(8,128)S(1)}, f32[5,3328]{1,0:T(8,128)}, u32[]{:S(2)}) copy-start(f32[5,3328]{1,0:T(8,128)} %param.46) | copy-start | bytes 199684
  1068.7 191.3 %copy-start.129 = (f32[48,48]{1,0:T(8,128)S(1)}, f32[48,48]{1,0:T(8,128)}, u32[]{:S(2)}) copy-start(f32[48,48]{1,0:T(8,128)} %param.41) | copy-start | bytes 27652
  1068.8 191.3 %copy-start.142 = (f32[48,48]{1,0:T(8,128)S(1)}, f32[48,48]{1,0:T(8,128)}, u32[]{:S(2)}) copy-start(f32[48,48]{1,0:T(8,128)} %param.42) | copy-start | bytes 27652
  1068.8 191.2 %copy-start.143 = (f32[48,48]{1,0:T(8,128)S(1)}, f32[48,48]{1,0:T(8,128)}, u32[]{:S(2)}) copy-start(f32[48,48]{1,0:T(8,128)} %param.43) | copy-start | bytes 27652
  1068.8 226.2 %copy-start.71 = (f32[384,384]{1,0:T(8,128)S(1)}, f32[384,384]{1,0:T(8,128)}, u32[]{:S(2)}) copy-start(f32[384,384]{1,0:T(8,128)} %param.53) | copy-start | bytes 1769476
  1068.8 226.2 %copy-start.81 = (f32[384,384]{1,0:T(8,128)S(1)}, f32[384,384]{1,0:T(8,128)}, u32[]{:S(2)}) copy-start(f32[384,384]{1,0:T(8,128)} %param.54) | copy-start | bytes 1769476
  1068.8 226.2 %copy-start.82 = (f32[384,384]{1,0:T(8,128)S(1)}, f32[384,384]{1,0:T(8,128)}, u32[]{:S(2)}) copy-start(f32[384,384]{1,0:T(8,128)} %param.55) | copy-start | bytes 1769476
  1069.6 228.0 %copy-start.136 = (f32[3072]{0:T(1024)}, f32[3072]{0:T(1024)S(1)}, u32[]{:S(2)}) copy-start(f32[3072]{0:T(1024)S(1)} %dynamic_update_slice.62) | copy-start | bytes 36868
  1069.7 190.3 %copy-start.151 = (f32[3,48]{1,0:T(4,128)}, f32[3,48]{1,0:T(4,128)S(1)}, u32[]{:S(2)}) copy-start(f32[3,48]{1,0:T(4,128)S(1)} %dynamic_update_slice.61) | copy-start | bytes 1732
  1261.4 137.3 %copy-start.115 = (f32[48,256]{1,0:T(8,128)S(1)}, f32[48,256]{1,0:T(8,128)}, u32[]{:S(2)}) copy-start(f32[48,256]{1,0:T(8,128)} %param.38) | copy-start | bytes 147460
  1261.4 137.3 %copy-start.137 = (f32[48,256]{1,0:T(8,128)S(1)}, f32[48,256]{1,0:T(8,128)}, u32[]{:S(2)}) copy-start(f32[48,256]{1,0:T(8,128)} %param.39) | copy-start | bytes 147460
  1261.4 137.3 %copy-start.138 = (f32[48,256]{1,0:T(8,128)S(1)}, f32[48,256]{1,0:T(8,128)}, u32[]{:S(2)}) copy-start(f32[48,256]{1,0:T(8,128)} %param.40) | copy-start | bytes 147460
  1261.4 187.4 %copy-start.61 = (f32[384,768]{1,0:T(8,128)S(1)}, f32[384,768]{1,0:T(8,128)}, u32[]{:S(2)}) copy-start(f32[384,768]{1,0:T(8,128)} %param.35) | copy-start | bytes 3538948
  1400.1 259.6 %copy-start.56 = (bf16[1536,256]{1,0:T(8,128)(2,1)S(1)}, bf16[1536,256]{1,0:T(8,128)(2,1)}, u32[]{:S(2)}) copy-start(bf16[1536,256]{1,0:T(8,128)(2,1)} %copy-done.55) | copy-start | bytes 2359300
  1400.1 259.6 %copy-start.78 = (f32[256,256]{1,0:T(8,128)S(1)}, f32[256,256]{1,0:T(8,128)}, u32[]{:S(2)}) copy-start(f32[256,256]{1,0:T(8,128)} %reduce-scatter.13.cloned.1.call-done) | copy-start | bytes 786436
  1453.2 208.4 %copy-start.44 = (bf16[256,1536]{1,0:T(8,128)(2,1)S(1)}, bf16[256,1536]{1,0:T(8,128)(2,1)}, u32[]{:S(2)}) copy-start(bf16[256,1536]{1,0:T(8,128)(2,1)} %param.30) | copy-start | bytes 2359300
  1453.2 208.4 %copy-start.63 = (bf16[1536,48]{1,0:T(8,128)(2,1)S(1)}, bf16[1536,48]{1,0:T(8,128)(2,1)}, u32[]{:S(2)}) copy-start(bf16[1536,48]{1,0:T(8,128)(2,1)} %copy-done.62) | copy-start | bytes 442372
  1453.2 208.4 %copy-start.111 = (f32[1536]{0:T(1024)S(1)}, f32[1536]{0:T(1024)}, u32[]{:S(2)}) copy-start(f32[1536]{0:T(1024)} %param.32) | copy-start | bytes 18436
  1661.6 209.2 %copy-start.66 = (bf16[256,1536]{1,0:T(8,128)(2,1)S(1)}, bf16[256,1536]{1,0:T(8,128)(2,1)}, u32[]{:S(2)}) copy-start(bf16[256,1536]{1,0:T(8,128)(2,1)} %param.31) | copy-start | bytes 2359300
  1706.4 167.8 %copy-start.148 = (f32[3072]{0:T(1024)}, f32[3072]{0:T(1024)S(1)}, u32[]{:S(2)}) copy-start(f32[3072]{0:T(1024)S(1)} %get-tuple-element.1713) | copy-start | bytes 36868
  1706.4 167.8 %copy-start.149 = (f32[1536]{0:T(1024)}, f32[1536]{0:T(1024)S(1)}, u32[]{:S(2)}) copy-start(f32[1536]{0:T(1024)S(1)} %get-tuple-element.1707) | copy-start | bytes 18436
  1706.4 167.8 %copy-start.153 = (f32[3,48]{1,0:T(4,128)}, f32[3,48]{1,0:T(4,128)S(1)}, u32[]{:S(2)}) copy-start(f32[3,48]{1,0:T(4,128)S(1)} %get-tuple-element.1712) | copy-start | bytes 1732
  (215 other events, 1012.0 us)
Sparse Core Ops, SparseCore 0:
  89.4 52.9 all-gather.6
  144.4 22.9 all-gather.4
  169.6 17.6 all-gather.8
  189.3 130.4 all-gather.10
  895.2 62.6 reduce-scatter.14
  961.3 67.3 reduce-scatter.12
  1034.8 121.7 all-reduce.37
  1162.8 97.1 reduce-scatter.20
  1263.1 31.8 reduce-scatter.22
  1300.7 97.9 reduce-scatter.18
  1401.8 47.0 reduce-scatter.16
  1452.3 207.4 reduce-scatter.10
  1663.3 207.4 reduce-scatter.8
